TPU v7x, 256 devices: a whole 4x4x8 slice. The times are simulated.
256 devices in a mesh: fsdp: 64 (over x_lo, z, y), dp: 4 (over x_hi, core).
Axes of the slice: x: 4 (x_hi: 2, x_lo: 2; x = x_hi * 2 + x_lo), y: 4, z: 8, core: 2. Of those that a mesh axis runs over, the one named last changes fastest.
Arguments:
- tokens: bfloat16 [4, 8192, 8192], P('dp', 'fsdp'), may hold values from -6 to 6
- queries: bfloat16 [4, 8192, 4096], P('dp', 'fsdp'), may hold values from -40 to 40, as said below
- keys: bfloat16 [4, 8192, 512], P('dp', 'fsdp'), may hold values from -4 to 4
- memory: bfloat16 [4, 8192, 8192], P('dp', 'fsdp'), may hold values from -6 to 6
- mem_keys: bfloat16 [4, 8192, 512], P('dp', 'fsdp'), may hold values from -4 to 4
- cotangent: bfloat16 [4, 8192, 4096], P('dp', 'fsdp'), may hold values from -6 to 6
- value_weight: bfloat16 [8192, 512], P('fsdp'), may hold values from -0.0625 to 0.0625
- dest_group: int32 [4, 128], P('dp', 'fsdp'), may hold values from 0 to 3, as said below
- source_group: int32 [4, 128], P('dp', 'fsdp'), may hold values from 0 to 3, as said below
- lengths: int32 [4, 128], P('dp', 'fsdp'), may hold values from 1 to 64
Outputs:
- grad_queries: bfloat16 [4, 8192, 4096], P('dp', 'fsdp')
- grad_keys: bfloat16 [4, 8192, 512], P('dp', 'fsdp')
- grad_memory: bfloat16 [4, 8192, 8192], P('dp', 'fsdp')
- grad_mem_keys: bfloat16 [4, 8192, 512], P('dp', 'fsdp')
- grad_weight: bfloat16 [8192, 512], P('fsdp')
Inputs may be any that keep to these rules, and one draw needn't show every extreme that they name: `queries`: large in the hidden draw where a query row copies its own key. `dest_group`: the 2 documents of a device go to two different groups, never its own; document k of every device of one fsdp index moves the same number of groups ahead. `source_group`: consistent with dest_group: every device receives exactly one document for each of its slots, at most one from each sender.
All inputs are finite; a program needn't handle non-finite values.
Results may differ from a plain program's by a relative error of at most 0.0075.
Values may be sent and summed in bfloat16 or wider, within the bound.
No kernel may reach another device: no remote copies, remote signals or barrier semaphores. Data moves between devices by JAX's collectives and lax.ppermute only.
A program may use at most 128 MiB of HBM per device.

v0:
```python
import jax
import jax.numpy as jnp
from jax import lax
from jax.sharding import PartitionSpec as P

HEAD_DIM = 128


def attend(query_rows, seg_keys, seg_values, slot_keys, slot_values, upstream, length):
    seg_len = query_rows.shape[0]
    mem_len = slot_keys.shape[0]
    kv_width = seg_keys.shape[1]
    heads_kv = kv_width // HEAD_DIM
    group_size = query_rows.shape[1] // kv_width
    key_count = seg_len + mem_len
    all_keys = jnp.concatenate([slot_keys, seg_keys], axis=0).reshape(key_count, heads_kv, HEAD_DIM)
    all_values = jnp.concatenate([slot_values, seg_values], axis=0).reshape(
        key_count, heads_kv, HEAD_DIM
    )
    query_heads = query_rows.reshape(seg_len, heads_kv, group_size, HEAD_DIM)
    score_scale = HEAD_DIM ** (-0.5)
    scores = (
        jnp.einsum("qkgd,jkd->kgqj", query_heads, all_keys, preferred_element_type=jnp.float32)
        * score_scale
    )
    positions = jnp.arange(seg_len)[:, None]
    columns = jnp.arange(key_count)[None, :]
    visible = (columns < mem_len) | (columns - mem_len <= positions)
    scores = jnp.where(visible, scores, -1e30)
    row_max = jnp.max(scores, axis=-1, keepdims=True)
    exp_scores = jnp.exp(scores - row_max)
    weights = exp_scores / jnp.sum(exp_scores, axis=-1, keepdims=True)
    weights_low = weights.astype(jnp.bfloat16)
    output = jnp.einsum(
        "kgqj,jkd->qkgd", weights_low, all_values, preferred_element_type=jnp.float32
    ).astype(jnp.bfloat16)
    live_rows = (jnp.arange(seg_len) < length).astype(jnp.bfloat16)
    masked = (
        upstream.reshape(seg_len, heads_kv, group_size, HEAD_DIM) * live_rows[:, None, None, None]
    )
    grad_weights = jnp.einsum(
        "qkgd,jkd->kgqj", masked, all_values, preferred_element_type=jnp.float32
    )
    grad_values = jnp.einsum(
        "kgqj,qkgd->jkd", weights_low, masked, preferred_element_type=jnp.float32
    ).reshape(key_count, kv_width)
    row_delta = jnp.einsum("qkgd,qkgd->kgq", masked, output, preferred_element_type=jnp.float32)
    grad_scores = (weights * (grad_weights - row_delta[..., None]) * score_scale).astype(
        jnp.bfloat16
    )
    grad_query = (
        jnp.einsum("kgqj,jkd->qkgd", grad_scores, all_keys, preferred_element_type=jnp.float32)
        .reshape(seg_len, -1)
        .astype(jnp.bfloat16)
    )
    grad_all_keys = jnp.einsum(
        "kgqj,qkgd->jkd", grad_scores, query_heads, preferred_element_type=jnp.float32
    ).reshape(key_count, kv_width)
    return (
        grad_query,
        grad_all_keys[:mem_len],
        grad_all_keys[mem_len:],
        grad_values[:mem_len],
        grad_values[mem_len:],
    )


def per_device(
    tokens,
    queries,
    keys,
    memory,
    mem_keys,
    cotangent,
    value_weight,
    dest_group,
    source_group,
    lengths,
):
    groups = lax.axis_size("dp")
    slot_count = dest_group.shape[1]
    seg_len = tokens.shape[1] // slot_count
    mem_len = memory.shape[1] // slot_count
    kv_width = value_weight.shape[1]
    model_width = tokens.shape[2]
    weight_full = lax.all_gather(value_weight, "fsdp", axis=0, tiled=True)
    stacked = jnp.concatenate([tokens[0], memory[0]], axis=0)
    values = jnp.dot(stacked, weight_full, preferred_element_type=jnp.float32).astype(jnp.bfloat16)
    split_at = slot_count * seg_len
    seg_values = values[:split_at].reshape(slot_count, seg_len, kv_width)
    doc_values = values[split_at:].reshape(slot_count, mem_len, kv_width)
    doc_keys = mem_keys[0].reshape(slot_count, mem_len, kv_width)
    targets = jnp.arange(groups, dtype=jnp.int32)
    send_table = (dest_group[0][None, :] == targets[:, None]).astype(jnp.bfloat16)
    take_table = (source_group[0][:, None] == targets[None, :]).astype(jnp.bfloat16)
    out_keys = jnp.einsum(
        "hs,smc->hmc", send_table, doc_keys, preferred_element_type=jnp.float32
    ).astype(jnp.bfloat16)
    out_values = jnp.einsum(
        "hs,smc->hmc", send_table, doc_values, preferred_element_type=jnp.float32
    ).astype(jnp.bfloat16)
    in_keys, in_values = (
        lax.all_to_all(out_keys, "dp", split_axis=0, concat_axis=0, tiled=True),
        lax.all_to_all(out_values, "dp", split_axis=0, concat_axis=0, tiled=True),
    )
    slot_keys = jnp.einsum(
        "sh,hmc->smc", take_table, in_keys, preferred_element_type=jnp.float32
    ).astype(jnp.bfloat16)
    slot_values = jnp.einsum(
        "sh,hmc->smc", take_table, in_values, preferred_element_type=jnp.float32
    ).astype(jnp.bfloat16)
    query_slots = queries[0].reshape(slot_count, seg_len, -1)
    key_slots = keys[0].reshape(slot_count, seg_len, kv_width)
    upstream_slots = cotangent[0].reshape(slot_count, seg_len, -1)
    grad_query, slot_grad_keys, seg_grad_keys, slot_grad_values, seg_grad_values = jax.vmap(attend)(
        query_slots, key_slots, seg_values, slot_keys, slot_values, upstream_slots, lengths[0]
    )
    back_keys = jnp.einsum(
        "sh,smc->hmc",
        take_table,
        slot_grad_keys.astype(jnp.bfloat16),
        preferred_element_type=jnp.float32,
    ).astype(jnp.bfloat16)
    back_values = jnp.einsum(
        "sh,smc->hmc",
        take_table,
        slot_grad_values.astype(jnp.bfloat16),
        preferred_element_type=jnp.float32,
    ).astype(jnp.bfloat16)
    ret_keys, ret_values = (
        lax.all_to_all(back_keys, "dp", split_axis=0, concat_axis=0, tiled=True),
        lax.all_to_all(back_values, "dp", split_axis=0, concat_axis=0, tiled=True),
    )
    doc_grad_keys = jnp.einsum(
        "hs,hmc->smc", send_table, ret_keys, preferred_element_type=jnp.float32
    ).astype(jnp.bfloat16)
    doc_grad_values = jnp.einsum(
        "hs,hmc->smc", send_table, ret_values, preferred_element_type=jnp.float32
    ).astype(jnp.bfloat16)
    doc_grad_flat = doc_grad_values.reshape(slot_count * mem_len, kv_width)
    grad_memory = lax.dot_general(
        doc_grad_flat, weight_full, (((1,), (1,)), ((), ())), preferred_element_type=jnp.float32
    ).astype(jnp.bfloat16)
    value_grads_all = jnp.concatenate(
        [seg_grad_values.astype(jnp.bfloat16).reshape(-1, kv_width), doc_grad_flat], axis=0
    )
    shares = lax.psum_scatter(
        lax.dot_general(
            stacked, value_grads_all, (((0,), (0,)), ((), ())), preferred_element_type=jnp.float32
        ),
        "fsdp",
        scatter_dimension=0,
        tiled=True,
    )
    grad_weight = lax.psum(shares, "dp").astype(jnp.bfloat16)
    return (
        grad_query.reshape(1, slot_count * seg_len, -1),
        seg_grad_keys.astype(jnp.bfloat16).reshape(1, slot_count * seg_len, kv_width),
        grad_memory.reshape(1, slot_count * mem_len, model_width),
        doc_grad_keys.reshape(1, slot_count * mem_len, kv_width),
        grad_weight,
    )


def solution(mesh):
    in_specs = (
        P("dp", "fsdp", None),
        P("dp", "fsdp", None),
        P("dp", "fsdp", None),
        P("dp", "fsdp", None),
        P("dp", "fsdp", None),
        P("dp", "fsdp", None),
        P("fsdp", None),
        P("dp", "fsdp"),
        P("dp", "fsdp"),
        P("dp", "fsdp"),
    )
    out_specs = (
        P("dp", "fsdp", None),
        P("dp", "fsdp", None),
        P("dp", "fsdp", None),
        P("dp", "fsdp", None),
        P("fsdp", None),
    )
    return jax.shard_map(
        per_device, mesh=mesh, in_specs=in_specs, out_specs=out_specs, check_vma=False
    )
```

profile of v0, /device:TPU:1, one launch (start us, length us, event | category | flops | bytes accessed | tf_op | source)
XLA Modules:
  0.0 706.9 jit_solution(6315596288376271972)
XLA Ops:
  8.1 1.1 convolution_convert_fusion.6
  10.0 7.2 %all-to-all-start = ((bf16[4,64,512]{2,1,0:T(8,128)(2,1)}), bf16[4,64,512]{2,1,0:T(8,128)(2,1)}, u32[]{:S(2)}, u32[]{:S(2)}) async-start(bf16[4,64,512]{2,1,0:T(8,128)(2,1)} %copy.35), calls=%async_computation | async-start | bytes 524288 | tf_op jit(solution)/shard_map/all_to_all | solution.py:103
  18.9 4.9 all-to-all-done
  23.8 1.3 convolution_convert_fusion.10
  25.3 2.3 fusion.70
  27.6 2.0 fusion.22
  31.4 1.1 copy.69
  33.6 5.0 all-to-all-start.2
  38.6 1.1 copy.71
  39.7 5.6 all-to-all-done.2
  45.3 1.3 convolution_convert_fusion.8
  46.6 10.4 %fusion.3 = f32[8192,512]{1,0:T(8,128)} fusion(bf16[128,8192]{1,0:T(8,128)(2,1)} %bitcast.133, bf16[128,8192]{1,0:T(8,128)(2,1)} %bitcast.135, bf16[128,512]{1,0:T(8,128)(2,1)S(1)} %bitcast.137, bf16[128,512]{1,0:T(8,128)(2,1)S(1)} %bitcast.145), kind=kOutput, calls=%fused_computation.5 | convolution fusion | flops 2156396544 | bytes 21233664 | tf_op jit(solution)/shard_map/dot_general | solution.py:148
  57.0 225.1 %all-gather.2.cloned.1.call-done = bf16[8192,512]{1,0:T(8,128)(2,1)} async-done(((bf16[128,512]{1,0:T(8,128)(2,1)}), bf16[8192,512]{1,0:T(8,128)(2,1)}) %all-gather.2.cloned.1.call-update) | async-done | bytes 8388624 | tf_op jit(solution)/shard_map/all_gather | solution.py:86
  282.1 7.0 fusion.14
  290.9 46.7 %all-to-all-start.1 = ((bf16[4,64,512]{2,1,0:T(8,128)(2,1)}), bf16[4,64,512]{2,1,0:T(8,128)(2,1)}, u32[]{:S(2)}, u32[]{:S(2)}) async-start(bf16[4,64,512]{2,1,0:T(8,128)(2,1)} %copy.41), calls=%async_computation.1 | async-start | bytes 524288 | tf_op jit(solution)/shard_map/all_to_all | solution.py:104
  337.6 7.5 %fusion.2 = bf16[1,128,8192]{2,1,0:T(8,128)(2,1)} fusion(bf16[128,512]{1,0:T(8,128)(2,1)S(1)} %bitcast.138, bf16[8192,512]{1,0:T(8,128)(2,1)} %all-gather.2.cloned.1.call-done), kind=kOutput, calls=%fused_computation.3 | convolution fusion | flops 1074790400 | bytes 10616832 | tf_op jit(solution)/shard_map/dot_general | solution.py:141
  346.1 1.3 convolution_convert_fusion.9
  349.1 2.2 fusion
  351.3 2.7 fusion.7
  356.3 4.8 all-to-all-start.3
  362.2 1.3 convert_element_type.86
  364.2 3.5 all-to-all-done.3
  368.7 264.8 %reduce-scatter.2.cloned.1.call-done = f32[128,512]{1,0:T(8,128)} async-done(((f32[8192,512]{1,0:T(8,128)}), f32[128,512]{1,0:T(8,128)}) %reduce-scatter.2.cloned.1.call-update) | async-done | bytes 262160 | tf_op jit(solution)/shard_map/reduce_scatter | solution.py:147
  633.5 66.5 %all-reduce.1 = bf16[128,512]{1,0:T(8,128)(2,1)} all-reduce(f32[128,512]{1,0:T(8,128)} %reduce-scatter.2.cloned.1.call-done), channel_id=1, replica_groups=mesh['fsdp'=64,'dp'=4] {'dp'}, use_global_device_ids=true, to_apply=%region_3.4 | all-reduce | flops 65536 | bytes 393216 | tf_op jit(solution)/shard_map/psum | solution.py:155
  (60 shorter events, 16.0 us)
Async XLA Ops:
  7.2 0.9 copy-start
  7.2 11.0 %copy-start.1 = (bf16[1,128,4096]{2,1,0:T(8,128)(2,1)S(1)}, bf16[1,128,4096]{2,1,0:T(8,128)(2,1)}, u32[]{:S(2)}) copy-start(bf16[1,128,4096]{2,1,0:T(8,128)(2,1)} %param.11) | copy-start | bytes 3145732
  7.2 274.9 %all-gather.2.cloned.1.call-start = ((), (), s32[]{:S(2)}) async-start(), calls=%async_computation.5 | async-start | bytes 8519680 | tf_op jit(solution)/shard_map/all_gather | solution.py:86
  8.1 10.4 %copy-start.2 = (bf16[1,128,4096]{2,1,0:T(8,128)(2,1)S(1)}, bf16[1,128,4096]{2,1,0:T(8,128)(2,1)}, u32[]{:S(2)}) copy-start(bf16[1,128,4096]{2,1,0:T(8,128)(2,1)} %param.15) | copy-start | bytes 3145732
  10.0 13.8 %all-to-all-start = ((bf16[4,64,512]{2,1,0:T(8,128)(2,1)}), bf16[4,64,512]{2,1,0:T(8,128)(2,1)}, u32[]{:S(2)}, u32[]{:S(2)}) async-start(bf16[4,64,512]{2,1,0:T(8,128)(2,1)} %copy.35), calls=%async_computation | async-start | bytes 524288 | tf_op jit(solution)/shard_map/all_to_all | solution.py:103
  18.1 7.1 %copy-start.3 = (bf16[2,64,4,128]{3,1,2,0:T(8,128)(2,1)}, bf16[2,64,4,128]{3,1,2,0:T(8,128)(2,1)S(1)}, u32[]{:S(2)}) copy-start(bf16[2,64,4,128]{3,1,2,0:T(8,128)(2,1)S(1)} %copy.38) | copy-start | bytes 393220
  18.2 0.7 copy-start.8
  18.2 5.7 copy-start.9
  25.3 2.3 copy-start.5
  27.6 2.9 copy-start.7
  30.5 14.8 %copy-start.10 = (s32[1,2]{1,0:T(1,128)S(1)}, s32[1,2]{1,0:T(1,128)}, u32[]{:S(2)}) copy-start(s32[1,2]{1,0:T(1,128)} %param.17) | copy-start | bytes 28
  33.6 11.6 %all-to-all-start.2 = ((bf16[4,64,512]{2,1,0:T(8,128)(2,1)}), bf16[4,64,512]{2,1,0:T(8,128)(2,1)}, u32[]{:S(2)}, u32[]{:S(2)}) async-start(bf16[4,64,512]{2,1,0:T(8,128)(2,1)} %copy.50), calls=%async_computation.2 | async-start | bytes 524288 | tf_op jit(solution)/shard_map/all_to_all | solution.py:132
  38.6 594.9 %reduce-scatter.2.cloned.1.call-start = ((), (), s32[]{:S(2)}) async-start(), calls=%async_computation.6 | async-start | bytes 17039360 | tf_op jit(solution)/shard_map/reduce_scatter | solution.py:147
  290.9 55.2 %all-to-all-start.1 = ((bf16[4,64,512]{2,1,0:T(8,128)(2,1)}), bf16[4,64,512]{2,1,0:T(8,128)(2,1)}, u32[]{:S(2)}, u32[]{:S(2)}) async-start(bf16[4,64,512]{2,1,0:T(8,128)(2,1)} %copy.41), calls=%async_computation.1 | async-start | bytes 524288 | tf_op jit(solution)/shard_map/all_to_all | solution.py:104
  354.8 6.3 copy-start.4
  354.8 6.3 copy-start.6
  356.3 11.4 %all-to-all-start.3 = ((bf16[4,64,512]{2,1,0:T(8,128)(2,1)}), bf16[4,64,512]{2,1,0:T(8,128)(2,1)S(1)}, u32[]{:S(2)}, u32[]{:S(2)}) async-start(bf16[4,64,512]{2,1,0:T(8,128)(2,1)} %copy.54), calls=%async_computation.3 | async-start | bytes 524288 | tf_op jit(solution)/shard_map/all_to_all | solution.py:131
Sparse Core Ops, SparseCore 0:
  9.8 272.2 all-gather.1
  284.6 348.8 reduce-scatter.1
where the time goes:
time: 708 us; the launch traced here: 707 us
  waiting for transfers between devices  505 us (71%)
  blocking collectives  66.5 us (9%)
  starting transfers between devices  63.7 us (9%)
  matrix products  40.8 us (6%)
  local copies, waits for them, and re-layouts  14.9 us (2%)
  between operations  14.4 us (2%)
    reduce_scatter x1, waiting for transfers between devices, per_device(): lax.psum_scatter(lax.dot_general(stacked, value_grads_all, (((0,), (0,)),...  265 us
    all_gather x1, waiting for transfers between devices, per_device(): weight_full = lax.all_gather(value_weight, 'fsdp', axis=0, tiled=True)  225 us
    psum x1, blocking collectives, per_device(): grad_weight = lax.psum(shares, 'dp').astype(jnp.bfloat16)  66.5 us
    all_to_all x1, starting transfers between devices, per_device(): lax.all_to_all(out_values, 'dp', split_axis=0, concat_axis=0, tiled=True)  46.7 us
  transfers between devices with their start and end apart: 6, of which 5 were waited for; matrix products, arithmetic and copies ran while one was open for 8% of the time, Pallas kernels for 0%

commit v1 on v0

--- a/solution.py
+++ b/solution.py
@@ -83,7 +83,9 @@
     mem_len = memory.shape[1] // slot_count
     kv_width = value_weight.shape[1]
     model_width = tokens.shape[2]
-    weight_full = lax.all_gather(value_weight, "fsdp", axis=0, tiled=True)
+    weight_full = jnp.concatenate(
+        lax.all_to_all(jnp.stack([value_weight] * lax.axis_size("fsdp")), "fsdp", 0, 0), axis=0
+    )
     stacked = jnp.concatenate([tokens[0], memory[0]], axis=0)
     values = jnp.dot(stacked, weight_full, preferred_element_type=jnp.float32).astype(jnp.bfloat16)
     split_at = slot_count * seg_len

time: 708 us -> 546 us (0.77)
  waiting for transfers between devices: 505 us -> 142 us
  blocking collectives: 66.5 us -> 317 us
  starting transfers between devices: 63.7 us -> 22.9 us
    all_to_all x0 -> x1, blocking collectives: none -> 272 us  [per_device(): lax.all_to_all(jnp.stack([value_weight] * lax.axis_size('fsdp')), 'fsdp',...]
    all_gather x1 -> x0, waiting for transfers between devices: 225 us -> none  [per_device(): weight_full = lax.all_gather(value_weight, 'fsdp', axis=0, tiled=True)]
    reduce_scatter x1, waiting for transfers between devices: 265 us -> 127 us  [per_device(): lax.psum_scatter(lax.dot_general(stacked, value_grads_all, (((0,), (0,)),...]
    all_to_all x1, starting transfers between devices: 46.7 us -> 6.56 us  [per_device(): lax.all_to_all(out_values, 'dp', split_axis=0, concat_axis=0, tiled=True)]
    psum x1, blocking collectives: 66.5 us -> 45.2 us  [per_device(): grad_weight = lax.psum(shares, 'dp').astype(jnp.bfloat16)]
  transfers between devices with their start and end apart: 6 -> 5, of which waited for: 5 -> 4; matrix products, arithmetic and copies ran while one was open for 8% -> 5% of each run, Pallas kernels for 0% -> 0%
where the time goes in v1:
time: 546 us; the launch traced here: 545 us
  blocking collectives  317 us (58%)
  waiting for transfers between devices  142 us (26%)
  matrix products  34.2 us (6%)
  starting transfers between devices  22.9 us (4%)
  between operations  14.4 us (3%)
  local copies, waits for them, and re-layouts  12 us (2%)
    all_to_all x1, blocking collectives, per_device(): lax.all_to_all(jnp.stack([value_weight] * lax.axis_size('fsdp')), 'fsdp',...  272 us
    reduce_scatter x1, waiting for transfers between devices, per_device(): lax.psum_scatter(lax.dot_general(stacked, value_grads_all, (((0,), (0,)),...  127 us
    psum x1, blocking collectives, per_device(): grad_weight = lax.psum(shares, 'dp').astype(jnp.bfloat16)  45.2 us
  transfers between devices with their start and end apart: 5, of which 4 were waited for; matrix products, arithmetic and copies ran while one was open for 5% of the time, Pallas kernels for 0%

profile of v1, /device:TPU:1, one launch (start us, length us, event | category | flops | bytes accessed | tf_op | source)
XLA Modules:
  0.0 544.5 jit_solution(8620923027837767879)
XLA Ops:
  8.1 1.1 convolution_convert_fusion.6
  9.9 7.2 %all-to-all-start = ((bf16[4,64,512]{2,1,0:T(8,128)(2,1)}), bf16[4,64,512]{2,1,0:T(8,128)(2,1)}, u32[]{:S(2)}, u32[]{:S(2)}) async-start(bf16[4,64,512]{2,1,0:T(8,128)(2,1)} %copy.35), calls=%async_computation | async-start | bytes 524288 | tf_op jit(solution)/shard_map/all_to_all | solution.py:105
  18.2 5.6 %all-to-all-done = bf16[4,64,512]{2,1,0:T(8,128)(2,1)} async-done(((bf16[4,64,512]{2,1,0:T(8,128)(2,1)}), bf16[4,64,512]{2,1,0:T(8,128)(2,1)}, u32[]{:S(2)}, u32[]{:S(2)}) %all-to-all-start) | async-done | bytes 262176 | tf_op jit(solution)/shard_map/all_to_all | solution.py:105
  23.7 1.3 convolution_convert_fusion.10
  25.2 2.3 fusion.70
  27.5 1.9 fusion.22
  29.4 0.9 fusion.13
  31.8 4.3 all-to-all-start.3
  36.3 6.4 %all-to-all-done.3 = bf16[4,64,512]{2,1,0:T(8,128)(2,1)S(1)} async-done(((bf16[4,64,512]{2,1,0:T(8,128)(2,1)}), bf16[4,64,512]{2,1,0:T(8,128)(2,1)S(1)}, u32[]{:S(2)}, u32[]{:S(2)}) %all-to-all-start.3) | async-done | bytes 262176 | tf_op jit(solution)/shard_map/all_to_all | solution.py:134
  43.1 10.3 %fusion.3 = f32[8192,512]{1,0:T(8,128)} fusion(bf16[128,8192]{1,0:T(8,128)(2,1)} %bitcast.136, bf16[128,8192]{1,0:T(8,128)(2,1)} %bitcast.138, bf16[128,512]{1,0:T(8,128)(2,1)S(1)} %bitcast.140, bf16[128,512]{1,0:T(8,128)(2,1)S(1)} %bitcast.148), kind=kOutput, calls=%fused_computation.5 | convolution fusion | flops 2156396544 | bytes 21233664 | tf_op jit(solution)/shard_map/dot_general | solution.py:150
  53.5 0.9 copy-done.8
  54.4 1.0 stack.2
  55.4 271.7 %all_to_all.25 = bf16[64,128,512]{2,1,0:T(8,128)(2,1)S(1)} all-to-all(bf16[64,128,512]{2,1,0:T(8,128)(2,1)S(1)} %stack.2), channel_id=1, replica_groups=mesh['fsdp'=64,'dp'=4] {'fsdp'}, dimensions={0} | all-to-all | bytes 16777216 | tf_op jit(solution)/shard_map/all_to_all | solution.py:87
  327.1 2.3 fusion.14
  329.5 0.9 copy-done.1
  331.5 6.6 %all-to-all-start.2 = ((bf16[4,64,512]{2,1,0:T(8,128)(2,1)}), bf16[4,64,512]{2,1,0:T(8,128)(2,1)S(1)}, u32[]{:S(2)}, u32[]{:S(2)}) async-start(bf16[4,64,512]{2,1,0:T(8,128)(2,1)} %copy.41), calls=%async_computation.2 | async-start | bytes 524288 | tf_op jit(solution)/shard_map/all_to_all | solution.py:106
  338.1 7.6 %fusion.2 = bf16[1,128,8192]{2,1,0:T(8,128)(2,1)} fusion(bf16[128,512]{1,0:T(8,128)(2,1)S(1)} %bitcast.141, bf16[8192,512]{1,0:T(8,128)(2,1)} %bitcast.132), kind=kOutput, calls=%fused_computation.3 | convolution fusion | flops 1074790400 | bytes 10616832 | tf_op jit(solution)/shard_map/dot_general | solution.py:143
  346.2 2.2 fusion
  348.4 2.8 fusion.7
  353.4 4.7 all-to-all-start.4
  359.3 1.3 convert_element_type.86
  361.4 3.5 all-to-all-done.4
  365.9 126.7 %reduce-scatter.2.cloned.1.call-done = f32[128,512]{1,0:T(8,128)} async-done(((f32[8192,512]{1,0:T(8,128)}), f32[128,512]{1,0:T(8,128)}) %reduce-scatter.2.cloned.1.call-update) | async-done | bytes 262160 | tf_op jit(solution)/shard_map/reduce_scatter | solution.py:149
  492.5 45.2 %all-reduce.1 = bf16[128,512]{1,0:T(8,128)(2,1)} all-reduce(f32[128,512]{1,0:T(8,128)} %reduce-scatter.2.cloned.1.call-done), channel_id=1, replica_groups=mesh['fsdp'=64,'dp'=4] {'dp'}, use_global_device_ids=true, to_apply=%region_3.4 | all-reduce | flops 65536 | bytes 393216 | tf_op jit(solution)/shard_map/psum | solution.py:157
  (63 shorter events, 11.6 us)
Async XLA Ops:
  7.2 0.9 copy-start
  7.2 9.9 %copy-start.4 = (bf16[1,128,4096]{2,1,0:T(8,128)(2,1)S(1)}, bf16[1,128,4096]{2,1,0:T(8,128)(2,1)}, u32[]{:S(2)}) copy-start(bf16[1,128,4096]{2,1,0:T(8,128)(2,1)} %param.15) | copy-start | bytes 3145732
  7.2 10.2 %copy-start.5 = (bf16[1,128,4096]{2,1,0:T(8,128)(2,1)S(1)}, bf16[1,128,4096]{2,1,0:T(8,128)(2,1)}, u32[]{:S(2)}) copy-start(bf16[1,128,4096]{2,1,0:T(8,128)(2,1)} %param.11) | copy-start | bytes 3145732
  9.9 13.9 %all-to-all-start = ((bf16[4,64,512]{2,1,0:T(8,128)(2,1)}), bf16[4,64,512]{2,1,0:T(8,128)(2,1)}, u32[]{:S(2)}, u32[]{:S(2)}) async-start(bf16[4,64,512]{2,1,0:T(8,128)(2,1)} %copy.35), calls=%async_computation | async-start | bytes 524288 | tf_op jit(solution)/shard_map/all_to_all | solution.py:105
  17.1 0.9 copy-start.9
  17.1 1.0 copy-start.10
  17.1 6.6 %copy-start.11 = (s32[1,2]{1,0:T(1,128)S(1)}, s32[1,2]{1,0:T(1,128)}, u32[]{:S(2)}) copy-start(s32[1,2]{1,0:T(1,128)} %param.18) | copy-start | bytes 28
  18.0 9.5 %copy-start.6 = (bf16[16,8,32,128]{3,2,1,0:T(8,128)(2,1)}, bf16[16,8,32,128]{3,2,1,0:T(8,128)(2,1)S(1)}, u32[]{:S(2)}) copy-start(bf16[16,8,32,128]{3,2,1,0:T(8,128)(2,1)S(1)} %copy.72) | copy-start | bytes 3145732
  30.4 12.4 %copy-start.12 = (s32[1,2]{1,0:T(1,128)S(1)}, s32[1,2]{1,0:T(1,128)}, u32[]{:S(2)}) copy-start(s32[1,2]{1,0:T(1,128)} %param.17) | copy-start | bytes 28
  31.8 10.9 %all-to-all-start.3 = ((bf16[4,64,512]{2,1,0:T(8,128)(2,1)}), bf16[4,64,512]{2,1,0:T(8,128)(2,1)S(1)}, u32[]{:S(2)}, u32[]{:S(2)}) async-start(bf16[4,64,512]{2,1,0:T(8,128)(2,1)} %copy.50), calls=%async_computation.3 | async-start | bytes 524288 | tf_op jit(solution)/shard_map/all_to_all | solution.py:134
  36.2 456.3 %reduce-scatter.2.cloned.1.call-start = ((), (), s32[]{:S(2)}) async-start(), calls=%async_computation.6 | async-start | bytes 17039360 | tf_op jit(solution)/shard_map/reduce_scatter | solution.py:149
  53.5 0.9 copy-start.8
  55.4 271.8 %copy-start.2 = (bf16[1,128,8192]{2,1,0:T(8,128)(2,1)S(1)}, bf16[1,128,8192]{2,1,0:T(8,128)(2,1)}, u32[]{:S(2)}) copy-start(bf16[1,128,8192]{2,1,0:T(8,128)(2,1)} %param.13) | copy-start | bytes 6291460
  55.4 271.8 %copy-start.3 = (bf16[1,128,8192]{2,1,0:T(8,128)(2,1)S(1)}, bf16[1,128,8192]{2,1,0:T(8,128)(2,1)}, u32[]{:S(2)}) copy-start(bf16[1,128,8192]{2,1,0:T(8,128)(2,1)} %param.10) | copy-start | bytes 6291460
  327.1 3.2 copy-start.1
  331.5 14.2 %all-to-all-start.2 = ((bf16[4,64,512]{2,1,0:T(8,128)(2,1)}), bf16[4,64,512]{2,1,0:T(8,128)(2,1)S(1)}, u32[]{:S(2)}, u32[]{:S(2)}) async-start(bf16[4,64,512]{2,1,0:T(8,128)(2,1)} %copy.41), calls=%async_computation.2 | async-start | bytes 524288 | tf_op jit(solution)/shard_map/all_to_all | solution.py:106
  348.4 2.8 copy-start.7
  353.4 11.4 %all-to-all-start.4 = ((bf16[4,64,512]{2,1,0:T(8,128)(2,1)}), bf16[4,64,512]{2,1,0:T(8,128)(2,1)S(1)}, u32[]{:S(2)}, u32[]{:S(2)}) async-start(bf16[4,64,512]{2,1,0:T(8,128)(2,1)} %copy.54), calls=%async_computation.4 | async-start | bytes 524288 | tf_op jit(solution)/shard_map/all_to_all | solution.py:133
Sparse Core Ops, SparseCore 0:
  53.6 438.8 reduce-scatter.1
